TPU v7x, 512 devices: a whole 4x4x16 slice. The times are simulated.
512 devices in a mesh: dp: 64 (over z, x_lo, core), tensor: 8 (over y, x_hi).
Axes of the slice: x: 4 (x_hi: 2, x_lo: 2; x = x_hi * 2 + x_lo), y: 4, z: 16, core: 2. Of those that a mesh axis runs over, the one named last changes fastest.
Arguments:
- hidden_in: bfloat16 [16384, 4096], P(('dp', 'tensor')), may hold values from -12 to 12
- norm_gain: bfloat16 [4096], replicated, may hold values from 0.5 to 1.5
- w_query: bfloat16 [4096, 4096], P('dp', 'tensor'), may hold values from -0.11328125 to 0.11328125
- w_key: bfloat16 [4096, 1024], P('dp', 'tensor'), may hold values from -0.11328125 to 0.11328125
- w_value: bfloat16 [4096, 1024], P('dp', 'tensor'), may hold values from -0.09375 to 0.09375
- w_out: bfloat16 [4096, 4096], P('tensor', 'dp'), may hold values from -0.09375 to 0.09375
- segment: int32 [16384], P('dp'), may hold values from -1 to 1, as said below
Outputs:
- hidden_out: bfloat16 [16384, 4096], P(('dp', 'tensor'))
- kv_cache: bfloat16 [16384, 8, 256], P('dp', 'tensor')
Inputs may be any that keep to these rules, and one draw needn't show every extreme that they name: `segment`: within each pack of 256 rows, prompts are numbered from 0 in order and each starts at a multiple of 128; a prompt's last tile may end in rows of -1, and whole tiles of -1 may only follow the last prompt of a pack; the first tile of every pack holds a prompt; in every draw some pack has no tile of -1 only and holds one prompt a tile.
All inputs are finite; a program needn't handle non-finite values.
Results may differ from a plain program's by a relative error of at most 0.0085.
Values may be sent and summed in bfloat16 or wider, within the bound.
No kernel may reach another device: no remote copies, remote signals or barrier semaphores. Data moves between devices by JAX's collectives and lax.ppermute only.
A program may use at most 64 MiB of HBM per device.

v0:
```python
import jax
import jax.numpy as jnp
from jax import lax
from jax.sharding import PartitionSpec as P

HEAD = 128
rope_theta = 500000.0
norm_epsilon = 1e-05


def inverse_frequency(head_width):
    exponent = jnp.arange(0, head_width, 2).astype(jnp.float32) / head_width
    base_freq = rope_theta ** (-exponent)
    wavelength = 2.0 * jnp.pi / base_freq
    smooth = (8192.0 / wavelength - 1.0) / 3.0
    blended = (1.0 - smooth) * base_freq / 8.0 + smooth * base_freq
    return jnp.where(
        wavelength < 2048.0, base_freq, jnp.where(wavelength > 8192.0, base_freq / 8.0, blended)
    )


def positions_of(segment):
    row_index = jnp.arange(segment.shape[0], dtype=jnp.int32)
    changed = jnp.concatenate([jnp.ones((1,), dtype=bool), segment[1:] != segment[:-1]])
    begins = lax.cummax(jnp.where(changed, row_index, 0), axis=0)
    return row_index - begins


def rotate(vectors, position):
    head_width = vectors.shape[-1]
    half_width = head_width // 2
    angles = position.astype(jnp.float32)[:, None] * inverse_frequency(head_width)[None, :]
    cosine = jnp.concatenate([jnp.cos(angles), jnp.cos(angles)], axis=-1)[:, None, :]
    sine_table = jnp.concatenate([jnp.sin(angles), jnp.sin(angles)], axis=-1)[:, None, :]
    turned = jnp.concatenate([-vectors[..., half_width:], vectors[..., :half_width]], axis=-1)
    return vectors * cosine + turned * sine_table


def rms_normed(rows_float, norm_gain):
    mean_square = jnp.mean(rows_float * rows_float, axis=-1, keepdims=True)
    return (
        rows_float * lax.rsqrt(mean_square + norm_epsilon) * norm_gain.astype(jnp.float32)
    ).astype(jnp.bfloat16)


def visible_pairs(segment, key_count):
    row_index = jnp.arange(segment.shape[0], dtype=jnp.int32)
    key_index = jnp.arange(key_count, dtype=jnp.int32)
    same_segment = (segment[:, None] == segment[None, :]) & (segment[:, None] >= 0)
    causal = key_index[None, :] <= row_index[:, None]
    return same_segment & causal | (key_index[None, :] == row_index[:, None])


def body(hidden_in, norm_gain, w_query, w_key, w_value, w_out, segment):
    pack_rows = segment.shape[0]
    query_cols = w_query.shape[1]
    kv_cols = w_key.shape[1]
    query_heads = query_cols // HEAD
    kv_heads = kv_cols // HEAD
    group_size = query_heads // kv_heads
    score_scale = HEAD ** (-0.5)
    rows_float = hidden_in.astype(jnp.float32)
    normed = rms_normed(rows_float, norm_gain)
    tensor_size = pack_rows // normed.shape[0]
    gathered = lax.all_to_all(
        jnp.broadcast_to(normed[None], (tensor_size,) + normed.shape), "tensor", 0, 0, tiled=True
    ).reshape(pack_rows, normed.shape[1])
    packed = jnp.concatenate((w_query, w_key, w_value, w_out.T), axis=1)
    packed_full = lax.all_gather(packed, "dp", axis=0, tiled=True)
    joined = packed_full[:, : query_cols + 2 * kv_cols]
    out_full_t = packed_full[:, query_cols + 2 * kv_cols :]
    projected = jnp.dot(gathered, joined, preferred_element_type=jnp.float32)
    position = positions_of(segment)
    query_rows = rotate(
        projected[:, :query_cols].reshape(pack_rows, query_heads, HEAD), position
    ).astype(jnp.bfloat16)
    key_rows = rotate(
        projected[:, query_cols : query_cols + kv_cols].reshape(pack_rows, kv_heads, HEAD), position
    ).astype(jnp.bfloat16)
    value_rows = (
        projected[:, query_cols + kv_cols :].astype(jnp.bfloat16).reshape(pack_rows, kv_heads, HEAD)
    )
    cache_rows = jnp.concatenate([key_rows, value_rows], axis=-1)
    grouped_query = query_rows.reshape(pack_rows, kv_heads, group_size, HEAD)
    scores = (
        jnp.einsum("skgh,tkh->kgst", grouped_query, key_rows, preferred_element_type=jnp.float32)
        * score_scale
    )
    allowed = visible_pairs(segment, pack_rows)
    scores = jnp.where(allowed, scores, -1e30)
    row_max = jnp.max(scores, axis=-1, keepdims=True)
    weight = jnp.exp(scores - row_max)
    weight_sum = jnp.sum(weight, axis=-1)
    mixed_rows = (
        jnp.einsum(
            "kgst,tkh->kgsh",
            weight.astype(jnp.bfloat16),
            value_rows,
            preferred_element_type=jnp.float32,
        )
        / weight_sum[..., None]
    )
    attended = (
        jnp.transpose(mixed_rows, (2, 0, 1, 3)).astype(jnp.bfloat16).reshape(pack_rows, query_cols)
    )
    out_rows = lax.dot_general(
        attended, out_full_t, (((1,), (1,)), ((), ())), preferred_element_type=jnp.float32
    )
    pieces = lax.all_to_all(
        out_rows.astype(jnp.bfloat16).reshape(tensor_size, -1, out_rows.shape[1]),
        "tensor",
        0,
        0,
        tiled=True,
    )
    summed = jnp.sum(pieces.astype(jnp.float32), axis=0)
    hidden_out = (summed + rows_float).astype(jnp.bfloat16)
    return (hidden_out, cache_rows)


def solution(mesh):
    return jax.shard_map(
        body,
        mesh=mesh,
        in_specs=(
            P(("dp", "tensor"), None),
            P(),
            P("dp", "tensor"),
            P("dp", "tensor"),
            P("dp", "tensor"),
            P("tensor", "dp"),
            P("dp"),
        ),
        out_specs=(P(("dp", "tensor"), None), P("dp", "tensor", None)),
        check_vma=False,
    )
```

profile of v0, /device:TPU:1, one launch (start us, length us, event | category | flops | bytes accessed | tf_op | source)
XLA Modules:
  0.0 200.9 jit_solution(4414675054207526265)
XLA Ops:
  7.2 1.6 pad_maximum_fusion
  8.8 0.7 convert_element_type.62
  9.5 1.1 fusion.8
  10.7 1.1 fusion.10
  11.7 1.5 broadcast_in_dim.13
  13.3 7.5 %all-to-all-start = ((bf16[8,32,4096]{2,1,0:T(8,128)(2,1)}), bf16[8,32,4096]{2,1,0:T(8,128)(2,1)S(1)}, u32[]{:S(2)}, u32[]{:S(2)}) async-start(bf16[8,32,4096]{2,1,0:T(8,128)(2,1)} %broadcast_in_dim.13), calls=%async_computation | async-start | bytes 4194304 | tf_op jit(solution)/shard_map/all_to_all | solution.py:65
  20.8 0.1 slice_compare_fusion
  20.8 0.1 fusion.27
  20.9 0.3 reduce-window.9
  21.2 0.1 slice.45
  21.4 0.1 slice_reduce_fusion
  21.5 0.1 fusion.28
  21.6 0.1 fusion.20
  21.7 0.5 multiply_cosine_fusion
  22.2 31.2 %all-to-all-done = bf16[8,32,4096]{2,1,0:T(8,128)(2,1)S(1)} async-done(((bf16[8,32,4096]{2,1,0:T(8,128)(2,1)}), bf16[8,32,4096]{2,1,0:T(8,128)(2,1)S(1)}, u32[]{:S(2)}, u32[]{:S(2)}) %all-to-all-start) | async-done | bytes 2097184 | tf_op jit(solution)/shard_map/all_to_all | solution.py:65
  53.4 94.2 %all-gather.2.cloned.1.call-done = bf16[4096,1280]{1,0:T(8,128)(2,1)} async-done(((bf16[64,1280]{1,0:T(8,128)(2,1)}), bf16[4096,1280]{1,0:T(8,128)(2,1)}) %all-gather.2.cloned.1.call-update) | async-done | bytes 10485776 | tf_op jit(solution)/shard_map/all_gather | solution.py:69
  147.6 4.6 %fusion = f32[256,768]{1,0:T(8,128)S(1)} fusion(bf16[256,4096]{1,0:T(8,128)(2,1)S(1)} %bitcast.71, bf16[4096,1280]{1,0:T(8,128)(2,1)} %all-gather.2.cloned.1.call-done), kind=kOutput, calls=%fused_computation | convolution fusion | flops 1610612736 | bytes 9175040 | tf_op jit(solution)/shard_map/dot_general | solution.py:72
  152.3 0.1 fusion.21
  152.4 0.2 reshape.137
  152.6 0.3 slice_negate_fusion
  152.9 0.2 fusion.23
  153.1 0.4 maximum_multiply_fusion
  153.5 0.1 mul.123
  153.6 0.4 fusion.29
  153.9 0.2 fusion.6
  154.1 0.3 fusion.5
  154.4 4.8 %convolution_convert_fusion = bf16[256,4096]{1,0:T(8,128)(2,1)} fusion(bf16[256,512]{0,1:T(8,128)(2,1)S(1)} %bitcast.77, bf16[4096,1280]{1,0:T(8,128)(2,1)} %all-gather.2.cloned.1.call-done), kind=kOutput, calls=%fused_computation.2 | convolution fusion | flops 1074790400 | bytes 6553600 | tf_op jit(solution)/shard_map/dot_general | solution.py:106
  159.2 5.8 %all-to-all-start.1 = ((bf16[8,32,4096]{2,1,0:T(8,128)(2,1)}), bf16[8,32,4096]{2,1,0:T(8,128)(2,1)S(1)}, u32[]{:S(2)}, u32[]{:S(2)}) async-start(bf16[8,32,4096]{2,1,0:T(8,128)(2,1)} %bitcast.72), calls=%async_computation.1 | async-start | bytes 4194304 | tf_op jit(solution)/shard_map/all_to_all | solution.py:109
  165.0 0.7 pad_maximum_fusion.3
  165.7 27.3 %all-to-all-done.1 = bf16[8,32,4096]{2,1,0:T(8,128)(2,1)S(1)} async-done(((bf16[8,32,4096]{2,1,0:T(8,128)(2,1)}), bf16[8,32,4096]{2,1,0:T(8,128)(2,1)S(1)}, u32[]{:S(2)}, u32[]{:S(2)}) %all-to-all-start.1) | async-done | bytes 2097184 | tf_op jit(solution)/shard_map/all_to_all | solution.py:109
  193.0 0.3 convert_reduce_fusion
  193.3 0.8 fusion.11
  (13 shorter events, 0.2 us)
Async XLA Ops:
  7.2 13.6 %copy-start.1 = (s32[256]{0:T(256)S(1)}, s32[256]{0:T(256)}, u32[]{:S(2)}) copy-start(s32[256]{0:T(256)} %param.13) | copy-start | bytes 3076
  7.2 140.5 %all-gather.2.cloned.1.call-start = ((), (), s32[]{:S(2)}) async-start(), calls=%async_computation.2 | async-start | bytes 10649600 | tf_op jit(solution)/shard_map/all_gather | solution.py:69
  13.3 40.1 %all-to-all-start = ((bf16[8,32,4096]{2,1,0:T(8,128)(2,1)}), bf16[8,32,4096]{2,1,0:T(8,128)(2,1)S(1)}, u32[]{:S(2)}, u32[]{:S(2)}) async-start(bf16[8,32,4096]{2,1,0:T(8,128)(2,1)} %broadcast_in_dim.13), calls=%async_computation | async-start | bytes 4194304 | tf_op jit(solution)/shard_map/all_to_all | solution.py:65
  159.2 34.0 %copy-start = (bf16[32,4096]{1,0:T(8,128)(2,1)S(1)}, bf16[32,4096]{1,0:T(8,128)(2,1)}, u32[]{:S(2)}) copy-start(bf16[32,4096]{1,0:T(8,128)(2,1)} %param.7) | copy-start | bytes 786436
  159.2 33.7 %all-to-all-start.1 = ((bf16[8,32,4096]{2,1,0:T(8,128)(2,1)}), bf16[8,32,4096]{2,1,0:T(8,128)(2,1)S(1)}, u32[]{:S(2)}, u32[]{:S(2)}) async-start(bf16[8,32,4096]{2,1,0:T(8,128)(2,1)} %bitcast.72), calls=%async_computation.1 | async-start | bytes 4194304 | tf_op jit(solution)/shard_map/all_to_all | solution.py:109
Sparse Core Ops, SparseCore 0:
  10.7 136.8 all-gather.1
where the time goes:
time: 201 us
  waiting for transfers between devices  153 us (76%)
  between operations  14.2 us (7%)
  starting transfers between devices  13.3 us (7%)
  matrix products  10 us (5%)
  other arithmetic  8.59 us (4%)
  local copies, waits for them, and re-layouts  2.09 us (1%)
    all_gather x1, waiting for transfers between devices, body(): packed_full = lax.all_gather(packed, 'dp', axis=0, tiled=True)  94.2 us
    all_to_all x1, waiting for transfers between devices, body(): lax.all_to_all(jnp.broadcast_to(normed[None], (tensor_size,) + normed.sha...  31.2 us
    all_to_all x1, waiting for transfers between devices, body(): lax.all_to_all(out_rows.astype(jnp.bfloat16).reshape(tensor_size, -1, out...  27.3 us
    all_to_all x1, starting transfers between devices, body(): lax.all_to_all(jnp.broadcast_to(normed[None], (tensor_size,) + normed.sha...  7.47 us
    all_to_all x1, starting transfers between devices, body(): lax.all_to_all(out_rows.astype(jnp.bfloat16).reshape(tensor_size, -1, out...  5.77 us
    dot_general x1, matrix products, body(): lax.dot_general(attended, out_full_t, (((1,), (1,)), ((), ())), preferred...  4.8 us
    dot_general x1, matrix products, body(): projected = jnp.dot(gathered, joined, preferred_element_type=jnp.float32)  4.56 us
  transfers between devices with their start and end apart: 3, of which 3 were waited for; matrix products, arithmetic and copies ran while one was open for 3% of the time, Pallas kernels for 0%

commit v1 on v0

--- a/solution.py
+++ b/solution.py
@@ -66,7 +66,10 @@
         jnp.broadcast_to(normed[None], (tensor_size,) + normed.shape), "tensor", 0, 0, tiled=True
     ).reshape(pack_rows, normed.shape[1])
     packed = jnp.concatenate((w_query, w_key, w_value, w_out.T), axis=1)
-    packed_full = lax.all_gather(packed, "dp", axis=0, tiled=True)
+    mixed_arr = jax.lax.psum(1, "dp")
+    spare = jnp.stack([packed] * mixed_arr)
+    part_now = jax.lax.all_to_all(spare, "dp", split_axis=0, concat_axis=0)
+    packed_full = jnp.concatenate(part_now, 0)
     joined = packed_full[:, : query_cols + 2 * kv_cols]
     out_full_t = packed_full[:, query_cols + 2 * kv_cols :]
     projected = jnp.dot(gathered, joined, preferred_element_type=jnp.float32)

time: 201 us -> 566 us (2.82)
  the two profiles are of different devices: /device:TPU:1 before, /device:TPU:34 now
where the time goes in v1:
time: 566 us; the launch traced here: 565 us
  waiting for transfers between devices  513 us (91%)
  starting transfers between devices  26.7 us (5%)
  matrix products  10 us (2%)
  local copies, waits for them, and re-layouts  7.26 us (1%)
  other arithmetic  7.07 us (1%)
    all_to_all x1, waiting for transfers between devices, body(): part_now = jax.lax.all_to_all(spare, 'dp', split_axis=0, concat_axis=0)  457 us
    all_to_all x1, waiting for transfers between devices, body(): lax.all_to_all(jnp.broadcast_to(normed[None], (tensor_size,) + normed.sha...  28.4 us
    all_to_all x1, waiting for transfers between devices, body(): lax.all_to_all(out_rows.astype(jnp.bfloat16).reshape(tensor_size, -1, out...  28.2 us
    all_to_all x1, starting transfers between devices, body(): part_now = jax.lax.all_to_all(spare, 'dp', split_axis=0, concat_axis=0)  17 us
  transfers between devices with their start and end apart: 3, of which 3 were waited for; matrix products, arithmetic and copies ran while one was open for 0% of the time, Pallas kernels for 0%

profile of v1, /device:TPU:34, one launch (start us, length us, event | category | flops | bytes accessed | tf_op | source)
XLA Modules:
  0.0 565.1 jit_solution(8455094510142542437)
XLA Ops:
  0.7 0.7 convert_element_type.62
  1.4 1.1 fusion.8
  2.5 1.1 fusion.10
  3.6 1.6 broadcast_in_dim.13
  5.2 6.0 %all-to-all-start = ((bf16[8,32,4096]{2,1,0:T(8,128)(2,1)}), bf16[8,32,4096]{2,1,0:T(8,128)(2,1)S(1)}, u32[]{:S(2)}, u32[]{:S(2)}) async-start(bf16[8,32,4096]{2,1,0:T(8,128)(2,1)} %broadcast_in_dim.13), calls=%async_computation | async-start | bytes 4194304 | tf_op jit(solution)/shard_map/all_to_all | solution.py:65
  11.3 28.4 %all-to-all-done = bf16[8,32,4096]{2,1,0:T(8,128)(2,1)S(1)} async-done(((bf16[8,32,4096]{2,1,0:T(8,128)(2,1)}), bf16[8,32,4096]{2,1,0:T(8,128)(2,1)S(1)}, u32[]{:S(2)}, u32[]{:S(2)}) %all-to-all-start) | async-done | bytes 2097184 | tf_op jit(solution)/shard_map/all_to_all | solution.py:65
  39.7 5.1 stack.2
  44.8 17.0 %all-to-all-start.1 = ((bf16[64,64,1280]{2,1,0:T(8,128)(2,1)}), bf16[64,64,1280]{2,1,0:T(8,128)(2,1)}, u32[]{:S(2)}, u32[]{:S(2)}) async-start(bf16[64,64,1280]{2,1,0:T(8,128)(2,1)} %stack.2), calls=%async_computation.1 | async-start | bytes 20971520 | tf_op jit(solution)/shard_map/all_to_all | solution.py:71
  61.8 0.1 slice_compare_fusion
  61.9 0.1 fusion.27
  62.0 0.3 reduce-window.9
  62.3 0.1 slice.45
  62.4 0.1 slice_reduce_fusion
  62.6 0.1 fusion.20
  62.7 0.5 multiply_cosine_fusion
  63.3 456.6 %all-to-all-done.1 = bf16[64,64,1280]{2,1,0:T(8,128)(2,1)} async-done(((bf16[64,64,1280]{2,1,0:T(8,128)(2,1)}), bf16[64,64,1280]{2,1,0:T(8,128)(2,1)}, u32[]{:S(2)}, u32[]{:S(2)}) %all-to-all-start.1) | async-done | bytes 10485792 | tf_op jit(solution)/shard_map/all_to_all | solution.py:71
  519.9 4.6 fusion
  524.5 0.1 fusion.21
  524.7 0.2 reshape.143
  524.9 0.3 slice_negate_fusion
  525.2 0.2 fusion.23
  525.4 0.4 maximum_multiply_fusion
  525.7 0.1 mul.123
  525.8 0.3 fusion.29
  526.2 0.2 fusion.6
  526.3 0.3 fusion.5
  526.7 4.8 convolution_convert_fusion
  531.5 3.7 all-to-all-start.2
  535.2 0.7 pad_maximum_fusion.3
  535.9 28.2 %all-to-all-done.2 = bf16[8,32,4096]{2,1,0:T(8,128)(2,1)S(1)} async-done(((bf16[8,32,4096]{2,1,0:T(8,128)(2,1)}), bf16[8,32,4096]{2,1,0:T(8,128)(2,1)S(1)}, u32[]{:S(2)}, u32[]{:S(2)}) %all-to-all-start.2) | async-done | bytes 2097184 | tf_op jit(solution)/shard_map/all_to_all | solution.py:112
  564.1 0.3 convert_reduce_fusion
  564.4 0.8 fusion.11
  (21 shorter events, 0.3 us)
Async XLA Ops:
  0.6 10.6 %copy-start.1 = (bf16[512,64]{0,1:T(8,128)(2,1)S(1)}, bf16[512,64]{0,1:T(8,128)(2,1)}, u32[]{:S(2)}) copy-start(bf16[512,64]{0,1:T(8,128)(2,1)} %param.12) | copy-start | bytes 196612
  0.6 10.6 %copy-start.4 = (bf16[64,128]{1,0:T(8,128)(2,1)S(1)}, bf16[64,128]{1,0:T(8,128)(2,1)}, u32[]{:S(2)}) copy-start(bf16[64,128]{1,0:T(8,128)(2,1)} %param.10) | copy-start | bytes 49156
  0.7 10.6 %copy-start.3 = (bf16[64,128]{1,0:T(8,128)(2,1)S(1)}, bf16[64,128]{1,0:T(8,128)(2,1)}, u32[]{:S(2)}) copy-start(bf16[64,128]{1,0:T(8,128)(2,1)} %param.11) | copy-start | bytes 49156
  0.7 10.6 %copy-start.2 = (bf16[64,512]{1,0:T(8,128)(2,1)S(1)}, bf16[64,512]{1,0:T(8,128)(2,1)}, u32[]{:S(2)}) copy-start(bf16[64,512]{1,0:T(8,128)(2,1)} %param.9) | copy-start | bytes 196612
  5.2 34.5 %all-to-all-start = ((bf16[8,32,4096]{2,1,0:T(8,128)(2,1)}), bf16[8,32,4096]{2,1,0:T(8,128)(2,1)S(1)}, u32[]{:S(2)}, u32[]{:S(2)}) async-start(bf16[8,32,4096]{2,1,0:T(8,128)(2,1)} %broadcast_in_dim.13), calls=%async_computation | async-start | bytes 4194304 | tf_op jit(solution)/shard_map/all_to_all | solution.py:65
  44.8 17.0 %copy-start.5 = (s32[256]{0:T(256)S(1)}, s32[256]{0:T(256)}, u32[]{:S(2)}) copy-start(s32[256]{0:T(256)} %param.13) | copy-start | bytes 3076
  44.8 475.1 %all-to-all-start.1 = ((bf16[64,64,1280]{2,1,0:T(8,128)(2,1)}), bf16[64,64,1280]{2,1,0:T(8,128)(2,1)}, u32[]{:S(2)}, u32[]{:S(2)}) async-start(bf16[64,64,1280]{2,1,0:T(8,128)(2,1)} %stack.2), calls=%async_computation.1 | async-start | bytes 20971520 | tf_op jit(solution)/shard_map/all_to_all | solution.py:71
  531.5 32.9 %copy-start = (bf16[32,4096]{1,0:T(8,128)(2,1)S(1)}, bf16[32,4096]{1,0:T(8,128)(2,1)}, u32[]{:S(2)}) copy-start(bf16[32,4096]{1,0:T(8,128)(2,1)} %param.7) | copy-start | bytes 786436
  531.5 32.6 %all-to-all-start.2 = ((bf16[8,32,4096]{2,1,0:T(8,128)(2,1)}), bf16[8,32,4096]{2,1,0:T(8,128)(2,1)S(1)}, u32[]{:S(2)}, u32[]{:S(2)}) async-start(bf16[8,32,4096]{2,1,0:T(8,128)(2,1)} %bitcast.73), calls=%async_computation.2 | async-start | bytes 4194304 | tf_op jit(solution)/shard_map/all_to_all | solution.py:112
